TPU v7x, 512 devices: a whole 4x4x16 slice. The times are simulated.
512 devices in a mesh: tiles: 32 (over z, core), chan: 16 (over y, x).
Axes of the slice: x: 4, y: 4, z: 16, core: 2. Of those that a mesh axis runs over, the one named last changes fastest.
Arguments:
- atmos_state: bfloat16 [256, 192, 256], P('tiles', 'chan'), may hold values from -6 to 6
- ocean_state: bfloat16 [256, 128, 256], P('tiles', 'chan'), may hold values from -6 to 6
- atmos_weight: bfloat16 [9, 192, 192], P(None, 'chan'), may hold values from -0.15625 to 0.15625
- ocean_weight: bfloat16 [9, 128, 128], P(None, 'chan'), may hold values from -0.1875 to 0.1875
- couple_weight: bfloat16 [128, 192], P('chan'), may hold values from -0.4375 to 0.4375
- sea_mask: int32 [256], replicated, may hold values from 0 to 1, as said below
- neighbours: int32 [256, 4], replicated, may hold values from 0 to 255, as said below
- rotations: int32 [256, 4], replicated, may hold values from 0 to 7
Outputs:
- atmos_next: bfloat16 [256, 192, 256], P('tiles', 'chan')
- ocean_next: bfloat16 [192, 128, 256], P('tiles', 'chan')
Inputs may be any that keep to these rules, and one draw needn't show every extreme that they name: `sea_mask`: exactly 192 of the 256 entries are 1; the tiles of blocks 2k and 2k + 1 of 8 tiles hold exactly 12 sea tiles together, and each such block holds between 4 and 8. neighbours[t, s] lies in the block of 8 tiles that holds t, or in the block just before or just after it, cyclically over the 32 blocks.
All inputs are finite; a program needn't handle non-finite values.
Results may differ from a plain program's by a relative error of at most 0.0034.
Values may be sent and summed in bfloat16 or wider, within the bound.
No kernel may reach another device: no remote copies, remote signals or barrier semaphores. Data moves between devices by JAX's collectives and lax.ppermute only.
A program may use at most 64 MiB of HBM per device.

v0:
```python
import jax
import jax.numpy as jnp
from jax import lax
from jax.sharding import PartitionSpec as P

SIDE = 16


def padded_2(cells, sides, width):
    for axis, dim in sides:
        count = lax.axis_size(axis)
        head = lax.slice_in_dim(cells, 0, width, axis=dim)
        tail = lax.slice_in_dim(cells, cells.shape[dim] - width, cells.shape[dim], axis=dim)
        cells = jnp.concatenate(
            [
                lax.ppermute(tail, axis, [(i, (i + 1) % count) for i in range(count)]),
                cells,
                lax.ppermute(head, axis, [((i + 1) % count, i) for i in range(count)]),
            ],
            axis=dim,
        )
    return cells


def partner(value, axis, distance):
    mask = 2**distance
    pairs = [(source, source ^ mask) for source in range(lax.axis_size(axis))]
    return lax.ppermute(value, axis, pairs)


def edge_set(tile_field):
    tile_count, chan_count = (tile_field.shape[0], tile_field.shape[1])
    tile_grid = tile_field.reshape(tile_count, chan_count, SIDE, SIDE)
    return jnp.stack(
        [
            tile_grid[:, :, 0, :],
            tile_grid[:, :, :, SIDE - 1],
            tile_grid[:, :, SIDE - 1, :],
            tile_grid[:, :, :, 0],
        ],
        axis=2,
    )


def pick_rims(edge_strips, adjacent, turn_codes):
    picked = edge_strips[adjacent]
    side_index = turn_codes % 4
    chosen = picked[:, :, :, 0, :]
    for edge_id in range(1, 4):
        chosen = jnp.where(
            (side_index == edge_id)[:, :, None, None], picked[:, :, :, edge_id, :], chosen
        )
    return jnp.where((turn_codes >= 4)[:, :, None, None], chosen[..., ::-1], chosen)


def pad_tile(tile_field, rim_cells):
    tile_count, chan_count = (tile_field.shape[0], tile_field.shape[1])
    tile_grid = tile_field.reshape(tile_count, chan_count, SIDE, SIDE)
    upper_row = jnp.pad(rim_cells[:, 0], ((0, 0), (0, 0), (1, 1)))[:, :, None, :]
    bottom = jnp.pad(rim_cells[:, 2], ((0, 0), (0, 0), (1, 1)))[:, :, None, :]
    middle = jnp.concatenate(
        [rim_cells[:, 3][:, :, :, None], tile_grid, rim_cells[:, 1][:, :, :, None]], axis=3
    )
    assembled = jnp.concatenate([upper_row, middle, bottom], axis=2).reshape(
        tile_count, chan_count, (SIDE + 2) * (SIDE + 2)
    )
    return jnp.pad(assembled, ((0, 0), (0, 0), (0, 2)))


def trim_columns(accum):
    tile_count, chan_count = (accum.shape[0], accum.shape[1])
    return accum.reshape(tile_count, chan_count, SIDE, SIDE + 2)[:, :, :, :SIDE].reshape(
        tile_count, chan_count, SIDE * SIDE
    )


def conv_step(weight, accum, piece):
    row_width = SIDE + 2
    out_span = SIDE * row_width
    for tap_index in range(9):
        offset = tap_index // 3 * row_width + tap_index % 3
        accum = accum + jnp.einsum(
            "oc,bcp->bop",
            weight[tap_index],
            piece[:, :, offset : offset + out_span],
            preferred_element_type=jnp.float32,
        )
    return accum


def ocean_layer(padded, forcing, own_state, ocean_weight, couple_weight):
    tile_count = padded.shape[0]
    out_chans = ocean_weight.shape[1]
    conv_start = jnp.zeros((tile_count, out_chans, SIDE * (SIDE + 2)), jnp.float32)
    conv_accum = conv_step(
        ocean_weight, conv_start, lax.all_gather(padded, "chan", axis=1, tiled=True)
    )
    couple_accum = jnp.einsum(
        "oc,bcp->bop",
        couple_weight,
        lax.all_gather(forcing, "chan", axis=1, tiled=True),
        preferred_element_type=jnp.float32,
    )
    mixed = trim_columns(conv_accum) + couple_accum
    return (own_state.astype(jnp.float32) + jax.nn.gelu(mixed, approximate=True)).astype(
        jnp.bfloat16
    )


def local(
    atmos_state,
    ocean_state,
    atmos_weight,
    ocean_weight,
    couple_weight,
    sea_mask,
    neighbours,
    rotations,
):
    per_dev = atmos_state.shape[0]
    atmos_local = atmos_state.shape[1]
    ocean_local = ocean_state.shape[1]
    groups = lax.axis_size("tiles")
    tile_group = lax.axis_index("tiles")
    first_tile = tile_group * per_dev
    sea_here = lax.dynamic_slice_in_dim(sea_mask, first_tile, per_dev, 0)
    sea_field = ocean_state * sea_here.astype(jnp.bfloat16)[:, None, None]
    edge_strips = jnp.concatenate([edge_set(atmos_state), edge_set(sea_field)], axis=1)
    widened = padded_2(edge_strips.reshape(per_dev, -1), (("tiles", 0),), per_dev)
    widened = widened.reshape(3 * per_dev, atmos_local + ocean_local, 4, SIDE)
    adjacent = lax.dynamic_slice_in_dim(neighbours, first_tile, per_dev, 0)
    turn_codes = lax.dynamic_slice_in_dim(rotations, first_tile, per_dev, 0)
    local_adjacent = (adjacent // per_dev - tile_group + 1) % groups * per_dev + adjacent % per_dev
    rim_cells = pick_rims(widened, local_adjacent, turn_codes)
    atmos_pad = pad_tile(atmos_state, rim_cells[:, :, :atmos_local])
    atmos_start = jnp.zeros((per_dev, atmos_weight.shape[1], SIDE * (SIDE + 2)), jnp.float32)
    atmos_accum = conv_step(
        atmos_weight, atmos_start, lax.all_gather(atmos_pad, "chan", axis=1, tiled=True)
    )
    atmos_next = (
        atmos_state.astype(jnp.float32) + jax.nn.gelu(trim_columns(atmos_accum), approximate=True)
    ).astype(jnp.bfloat16)
    per_owner = per_dev * 3 // 4
    ocean_total = per_owner * groups
    counts = jnp.sum(sea_mask.reshape(groups, per_dev), axis=1)
    starts = jnp.cumsum(counts) - counts
    sea_rank = jnp.cumsum(sea_mask) - 1
    rank_spots = jnp.where(sea_mask == 1, sea_rank, ocean_total)
    tile_of_rank = (
        jnp.zeros((ocean_total,), jnp.int32)
        .at[rank_spots]
        .set(jnp.arange(sea_mask.shape[0], dtype=jnp.int32), mode="drop")
    )
    my_first = starts[tile_group]
    my_last = my_first + counts[tile_group]
    parity = tile_group % 2
    pair_base = tile_group // 2 * 2 * per_owner
    slot_ids = jnp.arange(per_owner, dtype=jnp.int32)
    ranks_send = pair_base + 2 * slot_ids + (1 - parity)
    ranks_own = pair_base + 2 * slot_ids + parity
    send_tile = jnp.clip(tile_of_rank[ranks_send] - first_tile, 0, per_dev - 1)
    own_tile = jnp.clip(tile_of_rank[ranks_own] - first_tile, 0, per_dev - 1)
    from_here = (ranks_own >= my_first) & (ranks_own < my_last)
    block_width = (ocean_local + atmos_local) * SIDE * SIDE
    sea_block = jnp.concatenate([ocean_state, atmos_next], axis=1).reshape(per_dev, block_width)
    rim_flat = rim_cells[:, :, atmos_local:].reshape(per_dev, -1)
    packed = jnp.concatenate([sea_block, rim_flat], axis=1)
    received = partner(packed[send_tile], "tiles", 0)
    own_packed = jnp.where(from_here[:, None], packed[own_tile], received)
    own_block = own_packed[:, :block_width].reshape(
        per_owner, ocean_local + atmos_local, SIDE * SIDE
    )
    own_rims = own_packed[:, block_width:].reshape(per_owner, 4, ocean_local, SIDE)
    own_state = own_block[:, :ocean_local]
    ocean_next = ocean_layer(
        pad_tile(own_state, own_rims),
        own_block[:, ocean_local:],
        own_state,
        ocean_weight,
        couple_weight,
    )
    return (atmos_next, ocean_next)


def solution(mesh):
    placed = (
        P("tiles", "chan", None),
        P("tiles", "chan", None),
        P(None, "chan", None),
        P(None, "chan", None),
        P("chan", None),
        P(),
        P(),
        P(),
    )
    return jax.shard_map(
        local,
        mesh=mesh,
        in_specs=placed,
        out_specs=(P("tiles", "chan", None), P("tiles", "chan", None)),
        check_vma=False,
    )
```

profile of v0, /device:TPU:2, one launch (start us, length us, event | category | flops | bytes accessed | tf_op | source)
XLA Modules:
  0.0 114.3 jit_solution(959433694621876811)
XLA Ops:
  0.7 0.8 dynamic-slice_convert_fusion
  1.4 0.8 broadcast_multiply_fusion
  2.7 1.1 copy.100
  5.6 8.9 %collective-permute-start.1 = (bf16[8,1280]{1,0:T(8,128)(2,1)S(1)}, bf16[8,1280]{1,0:T(8,128)(2,1)S(1)}, u32[]{:S(2)}, u32[]{:S(2)}) collective-permute-start(bf16[8,1280]{1,0:T(8,128)(2,1)S(1)} %reshape.192), channel_id=1, source_target_pairs={{16,0},{32,16},{48,32},{64,48},{80,64},{96,80},{112,96},{128,112},... | collective-permute-start | bytes 61448 | tf_op jit(solution)/shard_map/ppermute | solution.py:18
  15.6 1.4 %scatter_custom_fusion = s32[192]{0:T(256)S(1)} fusion(s32[256]{0:T(256)S(1)} %compare_select_fusion.1, s32[256]{0:T(256)S(1)} %iota.13, s32[]{:T(128)} %constant.105.clone.1), kind=kCustom, calls=%fused_computation.181 | custom fusion | bytes 772 | tf_op jit(solution)/shard_map/scatter | solution.py:152
  17.0 0.6 gather_fusion.1
  17.6 0.6 gather_fusion.3
  18.5 0.6 dynamic_slice.19
  19.4 0.6 dynamic_slice.18
  22.4 0.6 gather_fusion
  24.0 0.5 pad_maximum_fusion
  24.5 1.6 %copy.122 = bf16[8,12,18,18]{3,2,0,1:T(8,128)(2,1)S(1)} copy(bf16[8,12,18,18]{1,3,2,0:T(8,128)(2,1)S(1)} %pad_maximum_fusion) | data formatting | bytes 124416 | tf_op jit(solution)/shard_map/concatenate | solution.py:64
  26.4 25.0 %all_gather.9 = bf16[8,192,326]{2,0,1:T(8,128)(2,1)S(1)} all-gather(bf16[8,12,326]{2,0,1:T(8,128)(2,1)S(1)} %pad.24), channel_id=1, replica_groups=mesh['tiles'=32,'chan'=16] {'chan'}, dimensions={1}, use_global_device_ids=true | all-gather | bytes 1064064 | tf_op jit(solution)/shard_map/all_gather | solution.py:138
  51.5 3.0 %fusion.131 = (bf16[8,192,288]{2,0,1:T(8,128)(2,1)S(1)}, bf16[8,192,288]{2,0,1:T(8,128)(2,1)S(1)}, bf16[8,192,288]{2,0,1:T(8,128)(2,1)S(1)}, bf16[8,192,288]{2,0...) fusion(bf16[8,192,326]{2,0,1:T(8,128)(2,1)S(1)} %all_gather.9), kind=kLoop, calls=%fused_computation.184 | loop fusion | bytes 15925248 | tf_op jit(solution)/shard_map/slice | solution.py:85
  57.0 0.5 reshape.194
  57.9 0.6 gather_fusion.4
  58.5 2.1 %collective-permute-start.2 = (bf16[6,5632]{1,0:T(8,128)(2,1)S(1)}, bf16[6,5632]{1,0:T(8,128)(2,1)S(1)}, u32[]{:S(2)}, u32[]{:S(2)}) collective-permute-start(bf16[6,5632]{1,0:T(8,128)(2,1)S(1)} %gather_fusion.4), channel_id=1, source_target_pairs={{0,16},{16,0},{32,48},{48,32},{64,80},{80,64},{96,112},{112,96},{1... | collective-permute-start | bytes 202760 | tf_op jit(solution)/shard_map/ppermute | solution.py:28
  60.6 0.7 compare_and_fusion
  61.3 0.6 gather_fusion.2
  62.7 0.4 copy.140
  63.1 0.4 copy.139
  63.4 0.4 pad_maximum_fusion.2
  64.1 22.6 %all_gather.10 = bf16[6,128,326]{2,1,0:T(8,128)(2,1)S(1)} all-gather(bf16[6,8,326]{2,1,0:T(8,128)(2,1)S(1)} %pad.27), channel_id=1, replica_groups=mesh['tiles'=32,'chan'=16] {'chan'}, dimensions={1}, use_global_device_ids=true | all-gather | bytes 532032 | tf_op jit(solution)/shard_map/all_gather | solution.py:96
  86.9 0.4 convolution_add_fusion.7
  87.2 0.4 convolution_add_fusion.6
  87.6 0.4 convolution_add_fusion.5
  87.9 0.4 convolution_add_fusion.4
  88.3 0.4 convolution_add_fusion.3
  88.6 0.4 convolution_add_fusion.2
  89.4 0.4 fusion.45
  90.2 23.3 %all_gather.11 = bf16[6,192,256]{2,0,1:T(8,128)(2,1)S(1)} all-gather(bf16[6,12,256]{2,0,1:T(8,128)(2,1)S(1)} %copy.153), channel_id=1, replica_groups=mesh['tiles'=32,'chan'=16] {'chan'}, dimensions={1}, use_global_device_ids=true | all-gather | bytes 626688 | tf_op jit(solution)/shard_map/all_gather | solution.py:101
  113.5 0.8 add_convert_fusion
  (116 shorter events, 10.7 us)
Async XLA Ops:
  0.6 112.9 %copy-start = (bf16[8,192]{1,0:T(8,128)(2,1)S(1)}, bf16[8,192]{1,0:T(8,128)(2,1)}, u32[]{:S(2)}) copy-start(bf16[8,192]{1,0:T(8,128)(2,1)} %param.12) | copy-start | bytes 9220
  2.7 11.9 %copy-start.5 = (s32[256]{0:T(256)S(1)}, s32[256]{0:T(256)}, u32[]{:S(2)}) copy-start(s32[256]{0:T(256)} %param.13) | copy-start | bytes 3076
  2.7 12.5 %copy-start.6 = (s32[256,4]{0,1:T(4,128)S(1)}, s32[256,4]{0,1:T(4,128)}, u32[]{:S(2)}) copy-start(s32[256,4]{0,1:T(4,128)} %param.14) | copy-start | bytes 12292
  2.7 12.7 %copy-start.7 = (s32[256,4]{0,1:T(4,128)S(1)}, s32[256,4]{0,1:T(4,128)}, u32[]{:S(2)}) copy-start(s32[256,4]{0,1:T(4,128)} %param.15) | copy-start | bytes 12292
  4.4 14.0 %copy-start.3 = (bf16[8,8,256]{2,1,0:T(8,128)(2,1)S(1)}, bf16[8,8,256]{2,1,0:T(8,128)(2,1)}, u32[]{:S(2)}) copy-start(bf16[8,8,256]{2,1,0:T(8,128)(2,1)} %param.9) | copy-start | bytes 98308
  5.6 16.2 %collective-permute-start.1 = (bf16[8,1280]{1,0:T(8,128)(2,1)S(1)}, bf16[8,1280]{1,0:T(8,128)(2,1)S(1)}, u32[]{:S(2)}, u32[]{:S(2)}) collective-permute-start(bf16[8,1280]{1,0:T(8,128)(2,1)S(1)} %reshape.192), channel_id=1, source_target_pairs={{16,0},{32,16},{48,32},{64,48},{80,64},{96,80},{112,96},{128,112},... | collective-permute-start | bytes 61448 | tf_op jit(solution)/shard_map/ppermute | solution.py:18
  14.5 6.8 %collective-permute-start = (bf16[8,1280]{1,0:T(8,128)(2,1)S(1)}, bf16[8,1280]{1,0:T(8,128)(2,1)S(1)}, u32[]{:S(2)}, u32[]{:S(2)}) collective-permute-start(bf16[8,1280]{1,0:T(8,128)(2,1)S(1)} %reshape.192), channel_id=1, source_target_pairs={{0,16},{16,32},{32,48},{48,64},{64,80},{80,96},{96,112},{112,128},... | collective-permute-start | bytes 61448 | tf_op jit(solution)/shard_map/ppermute | solution.py:16
  51.5 3.0 %copy-start.8 = (bf16[9,12,192]{2,1,0:T(8,128)(2,1)S(1)}, bf16[9,12,192]{2,1,0:T(8,128)(2,1)}, u32[]{:S(2)}) copy-start(bf16[9,12,192]{2,1,0:T(8,128)(2,1)} %param.10) | copy-start | bytes 124420
  56.9 0.9 copy-start.1
  57.9 4.1 %copy-start.2 = (bf16[8,12,256]{2,0,1:T(8,128)(2,1)}, bf16[8,12,256]{2,0,1:T(8,128)(2,1)S(1)}, u32[]{:S(2)}) copy-start(bf16[8,12,256]{2,0,1:T(8,128)(2,1)S(1)} %fusion.69) | copy-start | bytes 147460
  58.5 3.4 %collective-permute-start.2 = (bf16[6,5632]{1,0:T(8,128)(2,1)S(1)}, bf16[6,5632]{1,0:T(8,128)(2,1)S(1)}, u32[]{:S(2)}, u32[]{:S(2)}) collective-permute-start(bf16[6,5632]{1,0:T(8,128)(2,1)S(1)} %gather_fusion.4), channel_id=1, source_target_pairs={{0,16},{16,0},{32,48},{48,32},{64,80},{80,64},{96,112},{112,96},{1... | collective-permute-start | bytes 202760 | tf_op jit(solution)/shard_map/ppermute | solution.py:28
  62.7 24.0 %copy-start.4 = (bf16[9,8,128]{2,1,0:T(8,128)(2,1)S(1)}, bf16[9,8,128]{2,1,0:T(8,128)(2,1)}, u32[]{:S(2)}) copy-start(bf16[9,8,128]{2,1,0:T(8,128)(2,1)} %param.11) | copy-start | bytes 55300
where the time goes:
time: 115 us; the launch traced here: 114 us
  blocking collectives  71 us (62%)
  local copies, waits for them, and re-layouts  18.7 us (16%)
  starting transfers between devices  11.1 us (10%)
  matrix products  6.31 us (5%)
  other arithmetic  4.8 us (4%)
  between operations  2.53 us (2%)
    all_gather x1, blocking collectives, local(): lax.all_gather(atmos_pad, 'chan', axis=1, tiled=True)  25 us
    all_gather x1, blocking collectives, ocean_layer(): lax.all_gather(forcing, 'chan', axis=1, tiled=True)  23.3 us
    all_gather x1, blocking collectives, ocean_layer(): lax.all_gather(padded, 'chan', axis=1, tiled=True)  22.6 us
    ppermute x1, starting transfers between devices, padded_2(): lax.ppermute(head, axis, [((i + 1) % count, i) for i in range(count)])  8.95 us
    dot_general x18, matrix products, conv_step(): jnp.einsum('oc,bcp->bop', weight[tap_index], piece[:, :, offset:offset +...  5.48 us
    slice x1, local copies, waits for them, and re-layouts, conv_step(): piece[:, :, offset:offset + out_span]  2.97 us
  transfers between devices with their start and end apart: 3, of which 0 were waited for; matrix products, arithmetic and copies ran while one was open for 6% of the time, Pallas kernels for 0%

commit v1 on v0

--- a/solution.py
+++ b/solution.py
@@ -135,7 +135,11 @@
     atmos_pad = pad_tile(atmos_state, rim_cells[:, :, :atmos_local])
     atmos_start = jnp.zeros((per_dev, atmos_weight.shape[1], SIDE * (SIDE + 2)), jnp.float32)
     atmos_accum = conv_step(
-        atmos_weight, atmos_start, lax.all_gather(atmos_pad, "chan", axis=1, tiled=True)
+        atmos_weight,
+        atmos_start,
+        jnp.concatenate(
+            lax.all_to_all(jnp.stack([atmos_pad] * lax.axis_size("chan")), "chan", 0, 0), axis=1
+        ),
     )
     atmos_next = (
         atmos_state.astype(jnp.float32) + jax.nn.gelu(trim_columns(atmos_accum), approximate=True)

time: 115 us -> 110 us (0.957)
  blocking collectives: 71 us -> 45 us
  waiting for transfers between devices: 0.01 us -> 12.4 us
  starting transfers between devices: 11.1 us -> 18.7 us
    all_gather x1 -> x0, blocking collectives: 25 us -> none  [local(): lax.all_gather(atmos_pad, 'chan', axis=1, tiled=True)]
    all_to_all x0 -> x1, waiting for transfers between devices: none -> 8.87 us  [local(): lax.all_to_all(jnp.stack([atmos_pad] * lax.axis_size('chan')), 'chan', 0, 0)]
    all_to_all x0 -> x1, starting transfers between devices: none -> 7.61 us  [local(): lax.all_to_all(jnp.stack([atmos_pad] * lax.axis_size('chan')), 'chan', 0, 0)]
    ppermute x1, waiting for transfers between devices: 0.01 us -> 3.51 us  [padded_2(): lax.ppermute(tail, axis, [(i, (i + 1) % count) for i in range(count)])]
  transfers between devices with their start and end apart: 3 -> 4, of which waited for: 0 -> 2; matrix products, arithmetic and copies ran while one was open for 6% -> 7% of each run, Pallas kernels for 0% -> 0%
where the time goes in v1:
time: 110 us; the launch traced here: 109 us
  blocking collectives  45 us (41%)
  local copies, waits for them, and re-layouts  19.8 us (18%)
  starting transfers between devices  18.7 us (17%)
  waiting for transfers between devices  12.4 us (11%)
  matrix products  6.31 us (6%)
  other arithmetic  4.78 us (4%)
  between operations  2.54 us (2%)
    all_gather x1, blocking collectives, ocean_layer(): lax.all_gather(forcing, 'chan', axis=1, tiled=True)  22.6 us
    all_gather x1, blocking collectives, ocean_layer(): lax.all_gather(padded, 'chan', axis=1, tiled=True)  22.5 us
    ppermute x1, starting transfers between devices, padded_2(): lax.ppermute(head, axis, [((i + 1) % count, i) for i in range(count)])  8.95 us
    all_to_all x1, waiting for transfers between devices, local(): lax.all_to_all(jnp.stack([atmos_pad] * lax.axis_size('chan')), 'chan', 0, 0)  8.87 us
    all_to_all x1, starting transfers between devices, local(): lax.all_to_all(jnp.stack([atmos_pad] * lax.axis_size('chan')), 'chan', 0, 0)  7.61 us
    dot_general x18, matrix products, conv_step(): jnp.einsum('oc,bcp->bop', weight[tap_index], piece[:, :, offset:offset +...  5.48 us
    ppermute x1, waiting for transfers between devices, padded_2(): lax.ppermute(tail, axis, [(i, (i + 1) % count) for i in range(count)])  3.51 us
    slice x1, local copies, waits for them, and re-layouts, conv_step(): piece[:, :, offset:offset + out_span]  2.95 us
  transfers between devices with their start and end apart: 4, of which 2 were waited for; matrix products, arithmetic and copies ran while one was open for 7% of the time, Pallas kernels for 0%

profile of v1, /device:TPU:2, one launch (start us, length us, event | category | flops | bytes accessed | tf_op | source)
XLA Modules:
  0.0 109.5 jit_solution(18361998096521599721)
XLA Ops:
  0.7 0.8 dynamic-slice_convert_fusion
  1.4 0.8 broadcast_multiply_fusion
  2.7 1.1 %copy.119 = bf16[8,12,256]{1,2,0:T(8,128)(2,1)S(1)} copy(bf16[8,12,256]{2,0,1:T(8,128)(2,1)} %param.8) | data formatting | bytes 98304 | tf_op args[0]
  5.5 8.9 %collective-permute-start.1 = (bf16[8,1280]{1,0:T(8,128)(2,1)S(1)}, bf16[8,1280]{1,0:T(8,128)(2,1)S(1)}, u32[]{:S(2)}, u32[]{:S(2)}) collective-permute-start(bf16[8,1280]{1,0:T(8,128)(2,1)S(1)} %reshape.200), channel_id=1, source_target_pairs={{16,0},{32,16},{48,32},{64,48},{80,64},{96,80},{112,96},{128,112},... | collective-permute-start | bytes 61448 | tf_op jit(solution)/shard_map/ppermute | solution.py:18
  15.4 3.5 %collective-permute-done = bf16[8,1280]{1,0:T(8,128)(2,1)S(1)} collective-permute-done((bf16[8,1280]{1,0:T(8,128)(2,1)S(1)}, bf16[8,1280]{1,0:T(8,128)(2,1)S(1)}, u32[]{:S(2)}, u32[]{:S(2)}) %collective-permute-start) | collective-permute-done | bytes 20512 | tf_op jit(solution)/shard_map/ppermute | solution.py:16
  20.0 0.6 gather_fusion
  21.3 0.5 pad_maximum_fusion
  21.8 1.6 %copy.140 = bf16[8,12,18,18]{3,2,0,1:T(8,128)(2,1)S(1)} copy(bf16[8,12,18,18]{1,3,2,0:T(8,128)(2,1)S(1)} %pad_maximum_fusion) | data formatting | bytes 124416 | tf_op jit(solution)/shard_map/concatenate | solution.py:64
  23.7 1.1 %stack.8 = bf16[16,8,12,326]{3,1,2,0:T(8,128)(2,1)} broadcast(bf16[8,12,326]{2,0,1:T(8,128)(2,1)S(1)} %pad.24), dimensions={1,2,3} | broadcast | bytes 1064064 | tf_op jit(solution)/shard_map/stack | solution.py:141
  24.8 7.6 %all-to-all-start = ((bf16[16,8,12,326]{3,1,2,0:T(8,128)(2,1)}), bf16[16,8,12,326]{3,1,2,0:T(8,128)(2,1)S(1)}, u32[]{:S(2)}, u32[]{:S(2)}) async-start(bf16[16,8,12,326]{3,1,2,0:T(8,128)(2,1)} %stack.8), calls=%async_computation | async-start | bytes 2359296 | tf_op jit(solution)/shard_map/all_to_all | solution.py:141
  32.6 1.4 %scatter_custom_fusion = s32[192]{0:T(256)S(1)} fusion(s32[256]{0:T(256)S(1)} %compare_select_fusion.1, s32[256]{0:T(256)S(1)} %iota.13, s32[]{:T(128)} %constant.105.clone.1), kind=kCustom, calls=%fused_computation.181 | custom fusion | bytes 772 | tf_op jit(solution)/shard_map/scatter | solution.py:156
  34.1 0.6 gather_fusion.1
  34.7 0.6 gather_fusion.3
  35.5 0.6 dynamic_slice.19
  36.3 0.6 dynamic_slice.18
  38.7 8.9 %all-to-all-done = bf16[16,8,12,326]{3,1,2,0:T(8,128)(2,1)S(1)} async-done(((bf16[16,8,12,326]{3,1,2,0:T(8,128)(2,1)}), bf16[16,8,12,326]{3,1,2,0:T(8,128)(2,1)S(1)}, u32[]{:S(2)}, u32[]{:S(2)}) %all-to-all-start) | async-done | bytes 1001504 | tf_op jit(solution)/shard_map/all_to_all | solution.py:141
  47.5 3.0 %fusion.131 = (bf16[8,192,288]{2,0,1:T(8,128)(2,1)S(1)}, bf16[8,192,288]{2,0,1:T(8,128)(2,1)S(1)}, bf16[8,192,288]{2,0,1:T(8,128)(2,1)S(1)}, bf16[8,192,288]{2,0...) fusion(bf16[8,192,326]{2,0,1:T(8,128)(2,1)S(1)} %bitcast.185), kind=kLoop, calls=%fused_computation.184 | loop fusion | bytes 15925248 | tf_op jit(solution)/shard_map/slice | solution.py:85
  53.0 0.5 reshape.204
  54.0 0.6 gather_fusion.4
  54.6 2.1 %collective-permute-start.2 = (bf16[6,5632]{1,0:T(8,128)(2,1)S(1)}, bf16[6,5632]{1,0:T(8,128)(2,1)S(1)}, u32[]{:S(2)}, u32[]{:S(2)}) collective-permute-start(bf16[6,5632]{1,0:T(8,128)(2,1)S(1)} %gather_fusion.4), channel_id=1, source_target_pairs={{0,16},{16,0},{32,48},{48,32},{64,80},{80,64},{96,112},{112,96},{1... | collective-permute-start | bytes 202760 | tf_op jit(solution)/shard_map/ppermute | solution.py:28
  56.7 0.7 compare_and_fusion
  57.3 0.6 gather_fusion.2
  58.7 0.4 copy.158
  59.1 0.4 copy.157
  59.5 0.4 pad_maximum_fusion.2
  60.1 22.5 %all_gather.6 = bf16[6,128,326]{2,1,0:T(8,128)(2,1)S(1)} all-gather(bf16[6,8,326]{2,1,0:T(8,128)(2,1)S(1)} %pad.27), channel_id=1, replica_groups=mesh['tiles'=32,'chan'=16] {'chan'}, dimensions={1}, use_global_device_ids=true | all-gather | bytes 532032 | tf_op jit(solution)/shard_map/all_gather | solution.py:96
  82.8 0.4 convolution_add_fusion.7
  83.1 0.4 convolution_add_fusion.6
  83.5 0.4 convolution_add_fusion.5
  83.9 0.4 convolution_add_fusion.4
  86.1 22.6 %all_gather.7 = bf16[6,192,256]{2,0,1:T(8,128)(2,1)S(1)} all-gather(bf16[6,12,256]{2,0,1:T(8,128)(2,1)S(1)} %copy.171), channel_id=1, replica_groups=mesh['tiles'=32,'chan'=16] {'chan'}, dimensions={1}, use_global_device_ids=true | all-gather | bytes 626688 | tf_op jit(solution)/shard_map/all_gather | solution.py:101
  108.7 0.8 add_convert_fusion
  (118 shorter events, 11.7 us)
Async XLA Ops:
  0.6 108.0 %copy-start = (bf16[8,192]{1,0:T(8,128)(2,1)S(1)}, bf16[8,192]{1,0:T(8,128)(2,1)}, u32[]{:S(2)}) copy-start(bf16[8,192]{1,0:T(8,128)(2,1)} %param.12) | copy-start | bytes 9220
  2.7 11.8 %copy-start.5 = (s32[256]{0:T(256)S(1)}, s32[256]{0:T(256)}, u32[]{:S(2)}) copy-start(s32[256]{0:T(256)} %param.13) | copy-start | bytes 3076
  2.7 12.2 %copy-start.6 = (s32[256,4]{0,1:T(4,128)S(1)}, s32[256,4]{0,1:T(4,128)}, u32[]{:S(2)}) copy-start(s32[256,4]{0,1:T(4,128)} %param.14) | copy-start | bytes 12292
  2.7 12.5 %copy-start.7 = (s32[256,4]{0,1:T(4,128)S(1)}, s32[256,4]{0,1:T(4,128)}, u32[]{:S(2)}) copy-start(s32[256,4]{0,1:T(4,128)} %param.15) | copy-start | bytes 12292
  5.5 13.8 %collective-permute-start.1 = (bf16[8,1280]{1,0:T(8,128)(2,1)S(1)}, bf16[8,1280]{1,0:T(8,128)(2,1)S(1)}, u32[]{:S(2)}, u32[]{:S(2)}) collective-permute-start(bf16[8,1280]{1,0:T(8,128)(2,1)S(1)} %reshape.200), channel_id=1, source_target_pairs={{16,0},{32,16},{48,32},{64,48},{80,64},{96,80},{112,96},{128,112},... | collective-permute-start | bytes 61448 | tf_op jit(solution)/shard_map/ppermute | solution.py:18
  14.5 4.4 %collective-permute-start = (bf16[8,1280]{1,0:T(8,128)(2,1)S(1)}, bf16[8,1280]{1,0:T(8,128)(2,1)S(1)}, u32[]{:S(2)}, u32[]{:S(2)}) collective-permute-start(bf16[8,1280]{1,0:T(8,128)(2,1)S(1)} %reshape.200), channel_id=1, source_target_pairs={{0,16},{16,32},{32,48},{48,64},{64,80},{80,96},{96,112},{112,128},... | collective-permute-start | bytes 61448 | tf_op jit(solution)/shard_map/ppermute | solution.py:16
  24.8 7.8 %copy-start.3 = (bf16[8,8,256]{2,1,0:T(8,128)(2,1)S(1)}, bf16[8,8,256]{2,1,0:T(8,128)(2,1)}, u32[]{:S(2)}) copy-start(bf16[8,8,256]{2,1,0:T(8,128)(2,1)} %param.9) | copy-start | bytes 98308
  24.8 22.7 %all-to-all-start = ((bf16[16,8,12,326]{3,1,2,0:T(8,128)(2,1)}), bf16[16,8,12,326]{3,1,2,0:T(8,128)(2,1)S(1)}, u32[]{:S(2)}, u32[]{:S(2)}) async-start(bf16[16,8,12,326]{3,1,2,0:T(8,128)(2,1)} %stack.8), calls=%async_computation | async-start | bytes 2359296 | tf_op jit(solution)/shard_map/all_to_all | solution.py:141
  47.5 3.0 %copy-start.8 = (bf16[9,12,192]{2,1,0:T(8,128)(2,1)S(1)}, bf16[9,12,192]{2,1,0:T(8,128)(2,1)}, u32[]{:S(2)}) copy-start(bf16[9,12,192]{2,1,0:T(8,128)(2,1)} %param.10) | copy-start | bytes 124420
  53.0 0.9 copy-start.1
  53.9 4.1 %copy-start.2 = (bf16[8,12,256]{2,0,1:T(8,128)(2,1)}, bf16[8,12,256]{2,0,1:T(8,128)(2,1)S(1)}, u32[]{:S(2)}) copy-start(bf16[8,12,256]{2,0,1:T(8,128)(2,1)S(1)} %fusion.69) | copy-start | bytes 147460
  54.6 3.4 %collective-permute-start.2 = (bf16[6,5632]{1,0:T(8,128)(2,1)S(1)}, bf16[6,5632]{1,0:T(8,128)(2,1)S(1)}, u32[]{:S(2)}, u32[]{:S(2)}) collective-permute-start(bf16[6,5632]{1,0:T(8,128)(2,1)S(1)} %gather_fusion.4), channel_id=1, source_target_pairs={{0,16},{16,0},{32,48},{48,32},{64,80},{80,64},{96,112},{112,96},{1... | collective-permute-start | bytes 202760 | tf_op jit(solution)/shard_map/ppermute | solution.py:28
  58.7 23.9 %copy-start.4 = (bf16[9,8,128]{2,1,0:T(8,128)(2,1)S(1)}, bf16[9,8,128]{2,1,0:T(8,128)(2,1)}, u32[]{:S(2)}) copy-start(bf16[9,8,128]{2,1,0:T(8,128)(2,1)} %param.11) | copy-start | bytes 55300
